TPU v7x, 32 devices: a whole 2x2x4 slice. The times are simulated.
32 devices in a mesh: group: 2 (over y), sub: 4 (over z), tile: 2 (over x), rep: 2 (over core).
Axes of the slice: x: 2, y: 2, z: 4, core: 2. Of those that a mesh axis runs over, the one named last changes fastest.
Arguments:
- right_side: bfloat16 [16, 1024, 512], P(('group', 'sub', 'tile'), None, 'rep'), parts along dimension 0, may hold values from -6 to 6
- interface_inverse: bfloat16 [16, 1024, 1024], P(('group', 'sub', 'tile')), parts along dimension 0, may hold values from -0.1875 to 0.1875
- coupling: float32 [16, 2, 128], P(('group', 'sub', 'tile')), parts along dimension 0, may hold values from 0.5 to 2
- trace_rows: int32 [16, 2, 128], P(('group', 'sub', 'tile')), parts along dimension 0, may hold values from 0 to 1023
- deflation_basis: bfloat16 [16, 1024, 128], P(('group', 'sub', 'tile')), parts along dimension 0, may hold values from -0.375 to 0.375
- deflation_counts: int32 [16], P(('group', 'sub', 'tile')), parts along dimension 0, may hold values from 32 to 128, as said below
- coarse_inverse: bfloat16 [8, 2, 128, 4, 256], P('group', 'tile', 'rep', 'sub'), parts along dimension 0, may hold values from -0.25 to 0.25
Outputs:
- corrected_field: bfloat16 [16, 1024, 512], P(('group', 'sub', 'tile'), None, 'rep'), parts along dimension 0
There are 2 independent parts, one for each index of `group`. A program takes and returns all parts, laid end to end along the dimension named above; each array names one. Nothing has to cross between parts.
Inputs may be any that keep to these rules, and one draw needn't show every extreme that they name: `deflation_counts`: some subdomain has exactly 128 live deflation vectors.
All inputs are finite; a program needn't handle non-finite values.
Results may differ from a plain program's by a relative error of at most 0.035.
Values may be sent and summed in bfloat16 or wider, within the bound.
No kernel may reach another device: no remote copies, remote signals or barrier semaphores. Data moves between devices by JAX's collectives and lax.ppermute only.
A program may use at most 64 MiB of HBM per device.

v0:
```python
import jax
import jax.numpy as jnp
from jax import lax
from jax.sharding import PartitionSpec as P

ROUNDS = 2


def passed_along(shard, axis, by):
    peers = lax.axis_size(axis)
    pairs = [(i, i + by) for i in range(peers) if 0 <= i + by < peers]
    return lax.ppermute(shard, axis, pairs)


def add_columns(matrix, piece):
    return jnp.dot(matrix, piece, preferred_element_type=jnp.float32)


def local(
    right_side,
    interface_inverse,
    coupling,
    trace_rows,
    deflation_basis,
    deflation_counts,
    coarse_inverse,
):
    source = right_side[0].astype(jnp.float32)
    inverse = interface_inverse[0]
    iface_rows = inverse.shape[0]
    face_rows = coupling.shape[2]
    mode_cols = source.shape[1]
    slot_count = deflation_basis.shape[2]
    half_slots = coarse_inverse.shape[2]
    sub_count = lax.axis_size("sub")
    slot_ids = jnp.arange(slot_count, dtype=jnp.int32)
    masked_basis = jnp.where(
        slot_ids[None, :] < deflation_counts[0],
        deflation_basis[0],
        jnp.zeros((), deflation_basis.dtype),
    )
    coarse_block = coarse_inverse.reshape(sub_count * half_slots, coarse_inverse.shape[4])
    lower_gain = coupling[0, 0][:, None]
    upper_gain = coupling[0, 1][:, None]
    iterate = jnp.zeros((iface_rows, mode_cols), jnp.float32)
    for cycle_index in range(ROUNDS):
        lower_trace = iterate[trace_rows[0, 0]]
        upper_trace = iterate[trace_rows[0, 1]]
        from_lower = passed_along(upper_trace.astype(jnp.bfloat16), ("sub", "tile"), 1).astype(
            upper_trace.dtype
        )
        from_upper = passed_along(lower_trace.astype(jnp.bfloat16), ("sub", "tile"), -1).astype(
            lower_trace.dtype
        )
        lower_rows = source[:face_rows] + lower_gain * from_lower
        upper_rows = source[iface_rows - face_rows :] + upper_gain * from_upper
        boundary = jnp.concatenate(
            [lower_rows, source[face_rows : iface_rows - face_rows], upper_rows], axis=0
        ).astype(jnp.bfloat16)
        local_solve = jnp.dot(inverse, boundary, preferred_element_type=jnp.float32)
        defect = (local_solve - iterate).astype(jnp.bfloat16)
        projected = lax.dot_general(
            masked_basis, defect, (((0,), (0,)), ((), ())), preferred_element_type=jnp.float32
        ).astype(jnp.bfloat16)
        all_modes = lax.all_gather(projected, "rep", axis=1, tiled=True)
        partial_value = add_columns(
            coarse_block, lax.all_gather(all_modes, "tile", axis=0, tiled=True)
        )
        own_coarse = lax.psum_scatter(
            partial_value.astype(jnp.bfloat16), "sub", scatter_dimension=0, tiled=True
        )
        coarse_rows = lax.all_to_all(own_coarse, "rep", split_axis=1, concat_axis=0, tiled=True)
        iterate = local_solve + jnp.dot(
            masked_basis, coarse_rows, preferred_element_type=jnp.float32
        )
    return iterate.astype(jnp.bfloat16)[None]


def solution(mesh):
    placed = (
        P(("group", "sub", "tile"), None, "rep"),
        P(("group", "sub", "tile"), None, None),
        P(("group", "sub", "tile"), None, None),
        P(("group", "sub", "tile"), None, None),
        P(("group", "sub", "tile"), None, None),
        P(("group", "sub", "tile")),
        P("group", "tile", "rep", "sub", None),
    )
    return jax.shard_map(
        local,
        mesh=mesh,
        in_specs=placed,
        out_specs=P(("group", "sub", "tile"), None, "rep"),
        check_vma=False,
    )
```

profile of v0, /device:TPU:0, one launch (start us, length us, event | category | flops | bytes accessed | tf_op | source)
XLA Modules:
  0.0 124.2 jit_solution(14332137796741248323)
XLA Ops:
  8.3 4.8 %collective-permute-start = (bf16[128,256]{1,0:T(8,128)(2,1)S(1)}, bf16[128,256]{1,0:T(8,128)(2,1)S(1)}, u32[]{:S(2)}, u32[]{:S(2)}) collective-permute-start(bf16[128,256]{1,0:T(8,128)(2,1)S(1)} %gather_fusion), channel_id=1, source_target_pairs={{0,2},{2,4},{4,6},{6,8},{8,10},{10,12},{12,14},{1,3},{3,5},{5,7},{... | collective-permute-start | bytes 196616 | tf_op jit(solution)/shard_map/ppermute | solution.py:12
  14.0 1.3 %collective-permute-start.1 = (bf16[128,256]{1,0:T(8,128)(2,1)S(1)}, bf16[128,256]{1,0:T(8,128)(2,1)S(1)}, u32[]{:S(2)}, u32[]{:S(2)}) collective-permute-start(bf16[128,256]{1,0:T(8,128)(2,1)S(1)} %gather_fusion.1), channel_id=1, source_target_pairs={{2,0},{4,2},{6,4},{8,6},{10,8},{12,10},{14,12},{3,1},{5,3},{7,5},{... | collective-permute-start | bytes 196616 | tf_op jit(solution)/shard_map/ppermute | solution.py:12
  16.7 1.1 convert_element_type.57
  17.9 2.2 %collective-permute-done.1 = bf16[128,256]{1,0:T(8,128)(2,1)S(1)} collective-permute-done((bf16[128,256]{1,0:T(8,128)(2,1)S(1)}, bf16[128,256]{1,0:T(8,128)(2,1)S(1)}, u32[]{:S(2)}, u32[]{:S(2)}) %collective-permute-start.1) | collective-permute-done | bytes 65568 | tf_op jit(solution)/shard_map/ppermute | solution.py:12
  22.5 1.9 %all_gather.12 = bf16[128,512]{1,0:T(8,128)(2,1)S(1)} all-gather(bf16[128,256]{1,0:T(8,128)(2,1)S(1)} %convolution_convert_fusion.3), channel_id=1, replica_groups=mesh['group'=2,'sub'=4,'tile'=2,'rep'=2] {'rep'}, dimensions={1}, use_global_device_ids=true | all-gather | bytes 196608 | tf_op jit(solution)/shard_map/all_gather | solution.py:65
  24.4 6.9 %all_gather.13 = bf16[256,512]{1,0:T(8,128)(2,1)S(1)} all-gather(bf16[128,512]{1,0:T(8,128)(2,1)S(1)} %all_gather.12), channel_id=1, replica_groups=mesh['group'=2,'sub'=4,'tile'=2,'rep'=2] {'tile'}, dimensions={0}, use_global_device_ids=true | all-gather | bytes 393216 | tf_op jit(solution)/shard_map/all_gather | solution.py:67
  32.5 20.2 %reduce-scatter.7.cloned.1.call-done = bf16[64,512]{1,0:T(8,128)(2,1)} async-done(((bf16[256,512]{1,0:T(8,128)(2,1)}), bf16[64,512]{1,0:T(8,128)(2,1)}) %reduce-scatter.7.cloned.1.call-update) | async-done | bytes 65552
  53.7 3.8 %all_to_all.38 = bf16[64,2,256]{2,0,1:T(8,128)(2,1)S(1)} all-to-all(bf16[64,2,256]{2,0,1:T(8,128)(2,1)S(1)} %copy.35), channel_id=1, replica_groups=mesh['group'=2,'sub'=4,'tile'=2,'rep'=2] {'rep'}, dimensions={1} | all-to-all | bytes 131072 | tf_op jit(solution)/shard_map/all_to_all | solution.py:72
  57.5 1.6 %convolution_add_fusion.1 = f32[1024,256]{0,1:T(8,128)S(1)} fusion(f32[1024,256]{0,1:T(8,128)} %copy-done.1, bf16[128,256]{1,0:T(8,128)(2,1)S(1)} %bitcast.78, bf16[1,1024,128]{2,1,0:T(8,128)(2,1)S(1)} %copy-done.4, pred[128]{0:T(512)(128)(4,1)S(1)} %iota_compare_fusion), kind=kOutput, calls=%fused_computation.11 | convolution fusion | flops 67502080 | bytes 2424960 | tf_op jit(solution)/shard_map/dot_general | solution.py:73
  59.1 1.0 copy.37
  60.1 2.5 %gather_fusion.3 = bf16[128,256]{1,0:T(8,128)(2,1)} fusion(bf16[1024,256]{1,0:T(8,128)(2,1)} %copy.37, s32[1024]{0:T(1024)S(1)} %pad_clamp_fusion), kind=kCustom, calls=%fused_computation.3 | custom fusion | bytes 131584 | tf_op jit(solution)/shard_map/gather | solution.py:47
  62.6 2.5 %gather_fusion.2 = bf16[128,256]{1,0:T(8,128)(2,1)} fusion(bf16[1024,256]{1,0:T(8,128)(2,1)} %copy.37, s32[1024]{0:T(1024)S(1)} %pad_clamp_fusion.1), kind=kCustom, calls=%fused_computation.2 | custom fusion | bytes 131584 | tf_op jit(solution)/shard_map/gather | solution.py:48
  65.0 3.4 %collective-permute-start.2 = (bf16[128,256]{1,0:T(8,128)(2,1)}, bf16[128,256]{1,0:T(8,128)(2,1)S(1)}, u32[]{:S(2)}, u32[]{:S(2)}) collective-permute-start(bf16[128,256]{1,0:T(8,128)(2,1)} %gather_fusion.2), channel_id=1, source_target_pairs={{0,2},{2,4},{4,6},{6,8},{8,10},{10,12},{12,14},{1,3},{3,5},{5,7},{... | collective-permute-start | bytes 196616 | tf_op jit(solution)/shard_map/ppermute | solution.py:12
  68.5 1.3 %collective-permute-start.3 = (bf16[128,256]{1,0:T(8,128)(2,1)}, bf16[128,256]{1,0:T(8,128)(2,1)S(1)}, u32[]{:S(2)}, u32[]{:S(2)}) collective-permute-start(bf16[128,256]{1,0:T(8,128)(2,1)} %gather_fusion.3), channel_id=1, source_target_pairs={{2,0},{4,2},{6,4},{8,6},{10,8},{12,10},{14,12},{3,1},{5,3},{7,5},{... | collective-permute-start | bytes 196616 | tf_op jit(solution)/shard_map/ppermute | solution.py:12
  70.7 4.2 %collective-permute-done.3 = bf16[128,256]{1,0:T(8,128)(2,1)S(1)} collective-permute-done((bf16[128,256]{1,0:T(8,128)(2,1)}, bf16[128,256]{1,0:T(8,128)(2,1)S(1)}, u32[]{:S(2)}, u32[]{:S(2)}) %collective-permute-start.3) | collective-permute-done | bytes 65568 | tf_op jit(solution)/shard_map/ppermute | solution.py:12
  74.9 1.1 add_convert_fusion.1
  75.9 1.8 %fusion.7 = f32[1024,256]{0,1:T(8,128)S(1)} fusion(bf16[1,1024,1024]{2,1,0:T(8,128)(2,1)S(1)} %copy-done, bf16[768,256]{1,0:T(8,128)(2,1)} %copy-done.7, bf16[128,256]{1,0:T(8,128)(2,1)S(1)} %get-tuple-element.6, bf16[128,256]{1,0:T(8,128)(2,1)S(1)} %get-tuple-element.5), kind=kOutput, calls=%fused_computation.9 | convolution fusion | flops 538443776 | bytes 3670016 | tf_op jit(solution)/shard_map/dot_general | solution.py:60
  78.7 1.9 %all_gather.14 = bf16[128,512]{1,0:T(8,128)(2,1)S(1)} all-gather(bf16[128,256]{1,0:T(8,128)(2,1)S(1)} %convolution_convert_fusion.2), channel_id=1, replica_groups=mesh['group'=2,'sub'=4,'tile'=2,'rep'=2] {'rep'}, dimensions={1}, use_global_device_ids=true | all-gather | bytes 196608 | tf_op jit(solution)/shard_map/all_gather | solution.py:65
  80.6 6.4 %all_gather.15 = bf16[256,512]{1,0:T(8,128)(2,1)S(1)} all-gather(bf16[128,512]{1,0:T(8,128)(2,1)S(1)} %all_gather.14), channel_id=1, replica_groups=mesh['group'=2,'sub'=4,'tile'=2,'rep'=2] {'tile'}, dimensions={0}, use_global_device_ids=true | all-gather | bytes 393216 | tf_op jit(solution)/shard_map/all_gather | solution.py:67
  87.9 1.8 %copy.51 = bf16[256,512]{1,0:T(8,128)(2,1)} copy(bf16[256,512]{0,1:T(8,128)(2,1)} %fusion.13) | data formatting | bytes 524288
  89.7 18.1 %reduce-scatter.9.cloned.1.call-done = bf16[64,512]{1,0:T(8,128)(2,1)} async-done(((bf16[256,512]{1,0:T(8,128)(2,1)}), bf16[64,512]{1,0:T(8,128)(2,1)}) %reduce-scatter.9.cloned.1.call-update) | async-done | bytes 65552
  109.5 4.7 %all_to_all.39 = bf16[64,2,256]{2,0,1:T(8,128)(2,1)S(1)} all-to-all(bf16[64,2,256]{2,0,1:T(8,128)(2,1)} %copy.40), channel_id=1, replica_groups=mesh['group'=2,'sub'=4,'tile'=2,'rep'=2] {'rep'}, dimensions={1} | all-to-all | bytes 131072 | tf_op jit(solution)/shard_map/all_to_all | solution.py:72
  114.2 1.1 fusion.11
  115.3 2.0 %copy.42 = bf16[1,1024,256]{2,1,0:T(8,128)(2,1)} copy(bf16[1,1024,256]{1,2,0:T(8,128)(2,1)} %fusion.11) | data formatting | bytes 1048576 | tf_op jit(solution)/shard_map/broadcast_in_dim | solution.py:76
  (44 shorter events, 12.4 us)
Async XLA Ops:
  6.5 13.8 %copy-start = (bf16[1,1024,1024]{2,1,0:T(8,128)(2,1)S(1)}, bf16[1,1024,1024]{2,1,0:T(8,128)(2,1)}, u32[]{:S(2)}) copy-start(bf16[1,1024,1024]{2,1,0:T(8,128)(2,1)} %param.8) | copy-start | bytes 6291460
  6.5 46.1 %reduce-scatter.7.cloned.1.call-start = ((), (), s32[]{:S(2)}) async-start(), calls=%async_computation.4 | async-start | bytes 327680
  8.3 9.6 %collective-permute-start = (bf16[128,256]{1,0:T(8,128)(2,1)S(1)}, bf16[128,256]{1,0:T(8,128)(2,1)S(1)}, u32[]{:S(2)}, u32[]{:S(2)}) collective-permute-start(bf16[128,256]{1,0:T(8,128)(2,1)S(1)} %gather_fusion), channel_id=1, source_target_pairs={{0,2},{2,4},{4,6},{6,8},{8,10},{10,12},{12,14},{1,3},{3,5},{5,7},{... | collective-permute-start | bytes 196616 | tf_op jit(solution)/shard_map/ppermute | solution.py:12
  14.0 6.2 %collective-permute-start.1 = (bf16[128,256]{1,0:T(8,128)(2,1)S(1)}, bf16[128,256]{1,0:T(8,128)(2,1)S(1)}, u32[]{:S(2)}, u32[]{:S(2)}) collective-permute-start(bf16[128,256]{1,0:T(8,128)(2,1)S(1)} %gather_fusion.1), channel_id=1, source_target_pairs={{2,0},{4,2},{6,4},{8,6},{10,8},{12,10},{14,12},{3,1},{5,3},{7,5},{... | collective-permute-start | bytes 196616 | tf_op jit(solution)/shard_map/ppermute | solution.py:12
  16.7 3.6 %copy-start.8 = (f32[128]{0:T(128)}, f32[128]{0:T(128)S(1)}, u32[]{:S(2)}) copy-start(f32[128]{0:T(128)S(1)} %get-tuple-element.10) | copy-start | bytes 1540
  17.8 2.5 %copy-start.5 = (f32[1,1024,256]{2,1,0:T(8,128)}, f32[1,1024,256]{2,1,0:T(8,128)S(1)}, u32[]{:S(2)}) copy-start(f32[1,1024,256]{2,1,0:T(8,128)S(1)} %convert_element_type.57) | copy-start | bytes 3145732
  17.9 3.2 %copy-start.7 = (bf16[768,256]{1,0:T(8,128)(2,1)}, bf16[768,256]{1,0:T(8,128)(2,1)S(1)}, u32[]{:S(2)}) copy-start(bf16[768,256]{1,0:T(8,128)(2,1)S(1)} %fusion.23) | copy-start | bytes 1179652
  20.3 1.8 %copy-start.4 = (bf16[1,1024,128]{2,1,0:T(8,128)(2,1)S(1)}, bf16[1,1024,128]{2,1,0:T(8,128)(2,1)}, u32[]{:S(2)}) copy-start(bf16[1,1024,128]{2,1,0:T(8,128)(2,1)} %param.11) | copy-start | bytes 786436
  20.3 10.9 %copy-start.6 = (bf16[4,1,64,1,256]{4,2,3,1,0:T(8,128)(2,1)S(1)}, bf16[4,1,64,1,256]{4,2,3,1,0:T(8,128)(2,1)}, u32[]{:S(2)}) copy-start(bf16[4,1,64,1,256]{4,2,3,1,0:T(8,128)(2,1)} %param.13) | copy-start | bytes 393220
  21.1 1.0 copy-start.1
  32.4 75.4 %reduce-scatter.9.cloned.1.call-start = ((), (), s32[]{:S(2)}) async-start(), calls=%async_computation.5 | async-start | bytes 327680
  65.0 5.6 %collective-permute-start.2 = (bf16[128,256]{1,0:T(8,128)(2,1)}, bf16[128,256]{1,0:T(8,128)(2,1)S(1)}, u32[]{:S(2)}, u32[]{:S(2)}) collective-permute-start(bf16[128,256]{1,0:T(8,128)(2,1)} %gather_fusion.2), channel_id=1, source_target_pairs={{0,2},{2,4},{4,6},{6,8},{8,10},{10,12},{12,14},{1,3},{3,5},{5,7},{... | collective-permute-start | bytes 196616 | tf_op jit(solution)/shard_map/ppermute | solution.py:12
  68.5 6.4 %collective-permute-start.3 = (bf16[128,256]{1,0:T(8,128)(2,1)}, bf16[128,256]{1,0:T(8,128)(2,1)S(1)}, u32[]{:S(2)}, u32[]{:S(2)}) collective-permute-start(bf16[128,256]{1,0:T(8,128)(2,1)} %gather_fusion.3), channel_id=1, source_target_pairs={{2,0},{4,2},{6,4},{8,6},{10,8},{12,10},{14,12},{3,1},{5,3},{7,5},{... | collective-permute-start | bytes 196616 | tf_op jit(solution)/shard_map/ppermute | solution.py:12
  77.7 1.0 copy-start.2
  80.6 33.6 %copy-start.3 = (f32[1024,256]{0,1:T(8,128)S(1)}, f32[1024,256]{0,1:T(8,128)}, u32[]{:S(2)}) copy-start(f32[1024,256]{0,1:T(8,128)} %copy-done.2) | copy-start | bytes 3145732
Sparse Core Ops, SparseCore 0:
  32.5 20.0 reduce-scatter.6
  89.9 17.9 reduce-scatter.8
where the time goes:
time: 125 us; the launch traced here: 124 us
  waiting for transfers between devices  45.6 us (36%)
  blocking collectives  25.5 us (20%)
  local copies, waits for them, and re-layouts  17.6 us (14%)
  between operations  14.3 us (11%)
  starting transfers between devices  10.9 us (9%)
  matrix products  7.14 us (6%)
  other arithmetic  3.16 us (3%)
    unnamed x4, waiting for transfers between devices  38.3 us
    all_gather x2, blocking collectives, local(): lax.all_gather(all_modes, 'tile', axis=0, tiled=True)  13.3 us
    ppermute x4, starting transfers between devices, passed_along(): return lax.ppermute(shard, axis, pairs)  10.9 us
    all_to_all x2, blocking collectives, local(): lax.all_to_all(own_coarse, 'rep', split_axis=1, concat_axis=0, tiled=True)  8.49 us
    ppermute x4, waiting for transfers between devices, passed_along(): return lax.ppermute(shard, axis, pairs)  7.31 us
    unnamed x22, local copies, waits for them, and re-layouts  6.19 us
    all_gather x2, blocking collectives, local(): all_modes = lax.all_gather(projected, 'rep', axis=1, tiled=True)  3.79 us
    gather x2, local copies, waits for them, and re-layouts, local(): upper_trace = iterate[trace_rows[0, 1]]  3.33 us
  transfers between devices with their start and end apart: 6, of which 5 were waited for; matrix products, arithmetic and copies ran while one was open for 2% of the time, Pallas kernels for 0%

commit v1 on v0

--- a/solution.py
+++ b/solution.py
@@ -69,7 +69,10 @@
         own_coarse = lax.psum_scatter(
             partial_value.astype(jnp.bfloat16), "sub", scatter_dimension=0, tiled=True
         )
-        coarse_rows = lax.all_to_all(own_coarse, "rep", split_axis=1, concat_axis=0, tiled=True)
+        n_dev = lax.axis_size("rep")
+        blocks = jnp.stack(jnp.split(own_coarse, n_dev, axis=1), axis=0)
+        blocks = lax.all_to_all(blocks, "rep", split_axis=0, concat_axis=0)
+        coarse_rows = jnp.concatenate(blocks, axis=0)
         iterate = local_solve + jnp.dot(
             masked_basis, coarse_rows, preferred_element_type=jnp.float32
         )

time: 125 us -> 127 us (1.016)
  local copies, waits for them, and re-layouts: 17.6 us -> 18.9 us
    split x0 -> x2, local copies, waits for them, and re-layouts: none -> 1.56 us  [local(): blocks = jnp.stack(jnp.split(own_coarse, n_dev, axis=1), axis=0)]
    unnamed x22 -> x24, local copies, waits for them, and re-layouts: 6.19 us -> 5.94 us
where the time goes in v1:
time: 127 us; the launch traced here: 126 us
  waiting for transfers between devices  45.6 us (36%)
  blocking collectives  25.5 us (20%)
  local copies, waits for them, and re-layouts  18.9 us (15%)
  between operations  14.3 us (11%)
  starting transfers between devices  10.9 us (9%)
  matrix products  7.15 us (6%)
  other arithmetic  4.09 us (3%)
    unnamed x4, waiting for transfers between devices  38.3 us
    all_gather x2, blocking collectives, local(): lax.all_gather(all_modes, 'tile', axis=0, tiled=True)  13.3 us
    ppermute x4, starting transfers between devices, passed_along(): return lax.ppermute(shard, axis, pairs)  10.9 us
    all_to_all x2, blocking collectives, local(): blocks = lax.all_to_all(blocks, 'rep', split_axis=0, concat_axis=0)  8.49 us
    ppermute x4, waiting for transfers between devices, passed_along(): return lax.ppermute(shard, axis, pairs)  7.31 us
    unnamed x24, local copies, waits for them, and re-layouts  5.94 us
    all_gather x2, blocking collectives, local(): all_modes = lax.all_gather(projected, 'rep', axis=1, tiled=True)  3.79 us
    gather x2, local copies, waits for them, and re-layouts, local(): upper_trace = iterate[trace_rows[0, 1]]  3.33 us
  transfers between devices with their start and end apart: 6, of which 5 were waited for; matrix products, arithmetic and copies ran while one was open for 2% of the time, Pallas kernels for 0%

profile of v1, /device:TPU:0, one launch (start us, length us, event | category | flops | bytes accessed | tf_op | source)
XLA Modules:
  0.0 126.4 jit_solution(7237585949638254386)
XLA Ops:
  8.3 4.8 %collective-permute-start = (bf16[128,256]{1,0:T(8,128)(2,1)S(1)}, bf16[128,256]{1,0:T(8,128)(2,1)S(1)}, u32[]{:S(2)}, u32[]{:S(2)}) collective-permute-start(bf16[128,256]{1,0:T(8,128)(2,1)S(1)} %gather_fusion), channel_id=1, source_target_pairs={{0,2},{2,4},{4,6},{6,8},{8,10},{10,12},{12,14},{1,3},{3,5},{5,7},{... | collective-permute-start | bytes 196616 | tf_op jit(solution)/shard_map/ppermute | solution.py:12
  14.0 1.3 %collective-permute-start.1 = (bf16[128,256]{1,0:T(8,128)(2,1)S(1)}, bf16[128,256]{1,0:T(8,128)(2,1)S(1)}, u32[]{:S(2)}, u32[]{:S(2)}) collective-permute-start(bf16[128,256]{1,0:T(8,128)(2,1)S(1)} %gather_fusion.1), channel_id=1, source_target_pairs={{2,0},{4,2},{6,4},{8,6},{10,8},{12,10},{14,12},{3,1},{5,3},{7,5},{... | collective-permute-start | bytes 196616 | tf_op jit(solution)/shard_map/ppermute | solution.py:12
  16.7 1.1 convert_element_type.57
  17.9 2.2 %collective-permute-done.1 = bf16[128,256]{1,0:T(8,128)(2,1)S(1)} collective-permute-done((bf16[128,256]{1,0:T(8,128)(2,1)S(1)}, bf16[128,256]{1,0:T(8,128)(2,1)S(1)}, u32[]{:S(2)}, u32[]{:S(2)}) %collective-permute-start.1) | collective-permute-done | bytes 65568 | tf_op jit(solution)/shard_map/ppermute | solution.py:12
  22.4 1.9 %all_gather.12 = bf16[128,512]{1,0:T(8,128)(2,1)S(1)} all-gather(bf16[128,256]{1,0:T(8,128)(2,1)S(1)} %convolution_convert_fusion.3), channel_id=1, replica_groups=mesh['group'=2,'sub'=4,'tile'=2,'rep'=2] {'rep'}, dimensions={1}, use_global_device_ids=true | all-gather | bytes 196608 | tf_op jit(solution)/shard_map/all_gather | solution.py:65
  24.3 6.9 %all_gather.13 = bf16[256,512]{1,0:T(8,128)(2,1)S(1)} all-gather(bf16[128,512]{1,0:T(8,128)(2,1)S(1)} %all_gather.12), channel_id=1, replica_groups=mesh['group'=2,'sub'=4,'tile'=2,'rep'=2] {'tile'}, dimensions={0}, use_global_device_ids=true | all-gather | bytes 393216 | tf_op jit(solution)/shard_map/all_gather | solution.py:67
  32.4 20.2 %reduce-scatter.7.cloned.1.call-done = bf16[64,512]{1,0:T(8,128)(2,1)} async-done(((bf16[256,512]{1,0:T(8,128)(2,1)}), bf16[64,512]{1,0:T(8,128)(2,1)}) %reduce-scatter.7.cloned.1.call-update) | async-done | bytes 65552
  53.8 3.8 %all_to_all.10 = bf16[2,64,256]{2,1,0:T(8,128)(2,1)S(1)} all-to-all(bf16[2,64,256]{2,1,0:T(8,128)(2,1)S(1)} %copy.20), channel_id=1, replica_groups=mesh['group'=2,'sub'=4,'tile'=2,'rep'=2] {'rep'}, dimensions={0} | all-to-all | bytes 131072 | tf_op jit(solution)/shard_map/all_to_all | solution.py:74
  57.6 1.6 %convolution_add_fusion.1 = f32[1024,256]{0,1:T(8,128)S(1)} fusion(f32[1024,256]{0,1:T(8,128)} %copy-done.1, bf16[128,256]{1,0:T(8,128)(2,1)S(1)} %bitcast.78, bf16[1,1024,128]{2,1,0:T(8,128)(2,1)S(1)} %copy-done.4, pred[128]{0:T(512)(128)(4,1)S(1)} %iota_compare_fusion), kind=kOutput, calls=%fused_computation.11 | convolution fusion | flops 67502080 | bytes 2424960 | tf_op jit(solution)/shard_map/dot_general | solution.py:76
  59.2 1.0 copy.22
  60.2 2.5 %gather_fusion.3 = bf16[128,256]{1,0:T(8,128)(2,1)} fusion(bf16[1024,256]{1,0:T(8,128)(2,1)} %copy.22, s32[1024]{0:T(1024)S(1)} %pad_clamp_fusion), kind=kCustom, calls=%fused_computation.3 | custom fusion | bytes 131584 | tf_op jit(solution)/shard_map/gather | solution.py:47
  62.6 2.5 %gather_fusion.2 = bf16[128,256]{1,0:T(8,128)(2,1)} fusion(bf16[1024,256]{1,0:T(8,128)(2,1)} %copy.22, s32[1024]{0:T(1024)S(1)} %pad_clamp_fusion.1), kind=kCustom, calls=%fused_computation.2 | custom fusion | bytes 131584 | tf_op jit(solution)/shard_map/gather | solution.py:48
  65.1 3.5 %collective-permute-start.2 = (bf16[128,256]{1,0:T(8,128)(2,1)}, bf16[128,256]{1,0:T(8,128)(2,1)S(1)}, u32[]{:S(2)}, u32[]{:S(2)}) collective-permute-start(bf16[128,256]{1,0:T(8,128)(2,1)} %gather_fusion.2), channel_id=1, source_target_pairs={{0,2},{2,4},{4,6},{6,8},{8,10},{10,12},{12,14},{1,3},{3,5},{5,7},{... | collective-permute-start | bytes 196616 | tf_op jit(solution)/shard_map/ppermute | solution.py:12
  68.6 1.3 %collective-permute-start.3 = (bf16[128,256]{1,0:T(8,128)(2,1)}, bf16[128,256]{1,0:T(8,128)(2,1)S(1)}, u32[]{:S(2)}, u32[]{:S(2)}) collective-permute-start(bf16[128,256]{1,0:T(8,128)(2,1)} %gather_fusion.3), channel_id=1, source_target_pairs={{2,0},{4,2},{6,4},{8,6},{10,8},{12,10},{14,12},{3,1},{5,3},{7,5},{... | collective-permute-start | bytes 196616 | tf_op jit(solution)/shard_map/ppermute | solution.py:12
  70.8 4.2 %collective-permute-done.3 = bf16[128,256]{1,0:T(8,128)(2,1)S(1)} collective-permute-done((bf16[128,256]{1,0:T(8,128)(2,1)}, bf16[128,256]{1,0:T(8,128)(2,1)S(1)}, u32[]{:S(2)}, u32[]{:S(2)}) %collective-permute-start.3) | collective-permute-done | bytes 65568 | tf_op jit(solution)/shard_map/ppermute | solution.py:12
  75.0 1.1 add_convert_fusion.1
  76.0 1.8 %fusion.7 = f32[1024,256]{0,1:T(8,128)S(1)} fusion(bf16[1,1024,1024]{2,1,0:T(8,128)(2,1)S(1)} %copy-done, bf16[768,256]{1,0:T(8,128)(2,1)} %copy-done.7, bf16[128,256]{1,0:T(8,128)(2,1)S(1)} %get-tuple-element.6, bf16[128,256]{1,0:T(8,128)(2,1)S(1)} %get-tuple-element.5), kind=kOutput, calls=%fused_computation.9 | convolution fusion | flops 538443776 | bytes 3670016 | tf_op jit(solution)/shard_map/dot_general | solution.py:60
  78.8 1.9 %all_gather.14 = bf16[128,512]{1,0:T(8,128)(2,1)S(1)} all-gather(bf16[128,256]{1,0:T(8,128)(2,1)S(1)} %convolution_convert_fusion.2), channel_id=1, replica_groups=mesh['group'=2,'sub'=4,'tile'=2,'rep'=2] {'rep'}, dimensions={1}, use_global_device_ids=true | all-gather | bytes 196608 | tf_op jit(solution)/shard_map/all_gather | solution.py:65
  80.7 6.4 %all_gather.15 = bf16[256,512]{1,0:T(8,128)(2,1)S(1)} all-gather(bf16[128,512]{1,0:T(8,128)(2,1)S(1)} %all_gather.14), channel_id=1, replica_groups=mesh['group'=2,'sub'=4,'tile'=2,'rep'=2] {'tile'}, dimensions={0}, use_global_device_ids=true | all-gather | bytes 393216 | tf_op jit(solution)/shard_map/all_gather | solution.py:67
  88.0 1.8 %copy.31 = bf16[256,512]{1,0:T(8,128)(2,1)} copy(bf16[256,512]{0,1:T(8,128)(2,1)} %fusion.13) | data formatting | bytes 524288
  89.8 18.0 %reduce-scatter.9.cloned.1.call-done = bf16[64,512]{1,0:T(8,128)(2,1)} async-done(((bf16[256,512]{1,0:T(8,128)(2,1)}), bf16[64,512]{1,0:T(8,128)(2,1)}) %reduce-scatter.9.cloned.1.call-update) | async-done | bytes 65552
  111.7 4.7 %all_to_all.11 = bf16[2,64,256]{2,1,0:T(8,128)(2,1)S(1)} all-to-all(bf16[2,64,256]{2,1,0:T(8,128)(2,1)} %copy.24), channel_id=1, replica_groups=mesh['group'=2,'sub'=4,'tile'=2,'rep'=2] {'rep'}, dimensions={0} | all-to-all | bytes 131072 | tf_op jit(solution)/shard_map/all_to_all | solution.py:74
  116.4 1.1 fusion.11
  117.6 2.0 %copy.26 = bf16[1,1024,256]{2,1,0:T(8,128)(2,1)} copy(bf16[1,1024,256]{1,2,0:T(8,128)(2,1)} %fusion.11) | data formatting | bytes 1048576 | tf_op jit(solution)/shard_map/broadcast_in_dim | solution.py:79
  (50 shorter events, 14.6 us)
Async XLA Ops:
  6.5 13.8 %copy-start = (bf16[1,1024,1024]{2,1,0:T(8,128)(2,1)S(1)}, bf16[1,1024,1024]{2,1,0:T(8,128)(2,1)}, u32[]{:S(2)}) copy-start(bf16[1,1024,1024]{2,1,0:T(8,128)(2,1)} %param.8) | copy-start | bytes 6291460
  6.5 46.1 %reduce-scatter.7.cloned.1.call-start = ((), (), s32[]{:S(2)}) async-start(), calls=%async_computation.4 | async-start | bytes 327680
  8.3 9.6 %collective-permute-start = (bf16[128,256]{1,0:T(8,128)(2,1)S(1)}, bf16[128,256]{1,0:T(8,128)(2,1)S(1)}, u32[]{:S(2)}, u32[]{:S(2)}) collective-permute-start(bf16[128,256]{1,0:T(8,128)(2,1)S(1)} %gather_fusion), channel_id=1, source_target_pairs={{0,2},{2,4},{4,6},{6,8},{8,10},{10,12},{12,14},{1,3},{3,5},{5,7},{... | collective-permute-start | bytes 196616 | tf_op jit(solution)/shard_map/ppermute | solution.py:12
  14.0 6.2 %collective-permute-start.1 = (bf16[128,256]{1,0:T(8,128)(2,1)S(1)}, bf16[128,256]{1,0:T(8,128)(2,1)S(1)}, u32[]{:S(2)}, u32[]{:S(2)}) collective-permute-start(bf16[128,256]{1,0:T(8,128)(2,1)S(1)} %gather_fusion.1), channel_id=1, source_target_pairs={{2,0},{4,2},{6,4},{8,6},{10,8},{12,10},{14,12},{3,1},{5,3},{7,5},{... | collective-permute-start | bytes 196616 | tf_op jit(solution)/shard_map/ppermute | solution.py:12
  16.7 3.6 %copy-start.8 = (f32[128]{0:T(128)}, f32[128]{0:T(128)S(1)}, u32[]{:S(2)}) copy-start(f32[128]{0:T(128)S(1)} %get-tuple-element.14) | copy-start | bytes 1540
  17.8 2.5 %copy-start.5 = (f32[1,1024,256]{2,1,0:T(8,128)}, f32[1,1024,256]{2,1,0:T(8,128)S(1)}, u32[]{:S(2)}) copy-start(f32[1,1024,256]{2,1,0:T(8,128)S(1)} %convert_element_type.57) | copy-start | bytes 3145732
  17.9 3.2 %copy-start.7 = (bf16[768,256]{1,0:T(8,128)(2,1)}, bf16[768,256]{1,0:T(8,128)(2,1)S(1)}, u32[]{:S(2)}) copy-start(bf16[768,256]{1,0:T(8,128)(2,1)S(1)} %fusion.23) | copy-start | bytes 1179652
  20.3 1.8 %copy-start.4 = (bf16[1,1024,128]{2,1,0:T(8,128)(2,1)S(1)}, bf16[1,1024,128]{2,1,0:T(8,128)(2,1)}, u32[]{:S(2)}) copy-start(bf16[1,1024,128]{2,1,0:T(8,128)(2,1)} %param.11) | copy-start | bytes 786436
  20.3 10.9 %copy-start.6 = (bf16[4,1,64,1,256]{4,2,3,1,0:T(8,128)(2,1)S(1)}, bf16[4,1,64,1,256]{4,2,3,1,0:T(8,128)(2,1)}, u32[]{:S(2)}) copy-start(bf16[4,1,64,1,256]{4,2,3,1,0:T(8,128)(2,1)} %param.13) | copy-start | bytes 393220
  21.1 1.0 copy-start.1
  32.4 75.5 %reduce-scatter.9.cloned.1.call-start = ((), (), s32[]{:S(2)}) async-start(), calls=%async_computation.5 | async-start | bytes 327680
  65.1 5.7 %collective-permute-start.2 = (bf16[128,256]{1,0:T(8,128)(2,1)}, bf16[128,256]{1,0:T(8,128)(2,1)S(1)}, u32[]{:S(2)}, u32[]{:S(2)}) collective-permute-start(bf16[128,256]{1,0:T(8,128)(2,1)} %gather_fusion.2), channel_id=1, source_target_pairs={{0,2},{2,4},{4,6},{6,8},{8,10},{10,12},{12,14},{1,3},{3,5},{5,7},{... | collective-permute-start | bytes 196616 | tf_op jit(solution)/shard_map/ppermute | solution.py:12
  68.6 6.4 %collective-permute-start.3 = (bf16[128,256]{1,0:T(8,128)(2,1)}, bf16[128,256]{1,0:T(8,128)(2,1)S(1)}, u32[]{:S(2)}, u32[]{:S(2)}) collective-permute-start(bf16[128,256]{1,0:T(8,128)(2,1)} %gather_fusion.3), channel_id=1, source_target_pairs={{2,0},{4,2},{6,4},{8,6},{10,8},{12,10},{14,12},{3,1},{5,3},{7,5},{... | collective-permute-start | bytes 196616 | tf_op jit(solution)/shard_map/ppermute | solution.py:12
  77.8 1.0 copy-start.2
  80.7 35.8 %copy-start.3 = (f32[1024,256]{0,1:T(8,128)S(1)}, f32[1024,256]{0,1:T(8,128)}, u32[]{:S(2)}) copy-start(f32[1024,256]{0,1:T(8,128)} %copy-done.2) | copy-start | bytes 3145732
Sparse Core Ops, SparseCore 0:
  32.5 20.0 reduce-scatter.6
  90.0 17.8 reduce-scatter.8
